TPU v7x, 32 devices: a whole 2x2x4 slice. The times are simulated.
32 devices in a mesh: lat: 8 (over y, x, core), lon: 4 (over z).
Axes of the slice: x: 2, y: 2, z: 4, core: 2. Of those that a mesh axis runs over, the one named last changes fastest.
Arguments:
- spec_coef: bfloat16 [1280, 2, 64, 1280], P(('lat', 'lon')), may hold values from -0.119628906 to 0.119628906
- legendre: bfloat16 [1280, 128, 1280], P(('lat', 'lon')), may hold values from -0.15625 to 0.15625
- wave_ids: int32 [1280], replicated, may hold values from 0 to 1279, each once
- dep_drow: int32 [128, 5120], P('lat', 'lon'), may hold values from -1 to 1
- dep_dlon: int32 [128, 5120], P('lat', 'lon'), may hold values from -1 to 1
- dep_frac: float32 [2, 128, 5120], P(None, 'lat', 'lon'), may hold values from 0 to 1
Outputs:
- grid: bfloat16 [64, 128, 5120], P(None, 'lat', 'lon')
- departed: bfloat16 [64, 128, 5120], P(None, 'lat', 'lon')
Inputs may be any that keep to these rules, and one draw needn't show every extreme that they name: `wave_ids`: each zonal wavenumber 0 to 1279 stands in exactly one storage row.
All inputs are finite; a program needn't handle non-finite values.
Results may differ from a plain program's by a relative error of at most 0.0059.
Values may be sent and summed in bfloat16 or wider, within the bound.
No kernel may reach another device: no remote copies, remote signals or barrier semaphores. Data moves between devices by JAX's collectives and lax.ppermute only.
A program may use at most 128 MiB of HBM per device.

v0:
```python
import math
import jax
import jax.numpy as jnp
from jax import lax
from jax.sharding import PartitionSpec as P

REACH = 1


def padded_2(cells, sides, width, closed):
    for axis, dim in sides:
        count = lax.axis_size(axis)
        ends = count if closed else count - 1
        head = lax.slice_in_dim(cells, 0, width, axis=dim)
        tail = lax.slice_in_dim(cells, cells.shape[dim] - width, cells.shape[dim], axis=dim)
        cells = jnp.concatenate(
            [
                lax.ppermute(tail, axis, [(i, (i + 1) % count) for i in range(ends)]),
                cells,
                lax.ppermute(head, axis, [((i + 1) % count, i) for i in range(ends)]),
            ],
            axis=dim,
        )
    return cells


def wave_table(wave_order, lon_start, lon_count, cycle_size):
    longitude = lon_start + jnp.arange(lon_count, dtype=jnp.int32)
    phase_index = wave_order[:, None] * longitude[None, :] % cycle_size
    theta = phase_index.astype(jnp.float32) * (2.0 * math.pi / cycle_size)
    factor = jnp.where(wave_order == 0, 1.0, 2.0).astype(jnp.float32)[:, None]
    return jnp.stack([factor * jnp.cos(theta), -factor * jnp.sin(theta)]).astype(jnp.bfloat16)


def shift_weight(offsets, frac, shift):
    zeros = jnp.zeros_like(frac)
    lower = jnp.where(offsets == shift, 1.0 - frac, zeros)
    higher = jnp.where(offsets == shift - 1, frac, zeros)
    return lower + higher


def per_device(spec_coef, legendre, wave_ids, dep_drow, dep_dlon, dep_frac):
    lat_count = lax.axis_size("lat")
    lon_parts = lax.axis_size("lon")
    local_waves = spec_coef.shape[0]
    level_fields = spec_coef.shape[2]
    degree_count = spec_coef.shape[3]
    all_waves = wave_ids.shape[0]
    row_count = dep_drow.shape[0]
    sector_width = dep_drow.shape[1]
    cycle_size = sector_width * lon_parts
    quarter = level_fields // lon_parts
    device = lax.axis_index("lat") * lon_parts + lax.axis_index("lon")
    local_ids = lax.dynamic_slice_in_dim(wave_ids, device * local_waves, local_waves)
    keep = jnp.arange(degree_count, dtype=jnp.int32)[None, :] >= local_ids[:, None]
    kept = jnp.where(keep[:, None, None, :], spec_coef, jnp.zeros((), spec_coef.dtype))
    kept = kept.reshape(local_waves, 2, lon_parts, quarter, degree_count)
    matrices = legendre.reshape(local_waves, lat_count, row_count, degree_count)
    fourier = jnp.einsum(
        "mrbqn,mapn->mabprq", kept, matrices, preferred_element_type=jnp.float32
    ).astype(jnp.bfloat16)
    moved = lax.all_to_all(
        lax.all_to_all(fourier, "lat", split_axis=1, concat_axis=0, tiled=True),
        "lon",
        split_axis=2,
        concat_axis=0,
        tiled=True,
    )
    wave_order = (
        wave_ids.reshape(lat_count, lon_parts, local_waves).transpose(1, 0, 2).reshape(all_waves)
    )
    moved = moved.reshape(all_waves, row_count, 2, quarter)
    table = wave_table(wave_order, lax.axis_index("lon") * sector_width, sector_width, cycle_size)
    grid = jnp.einsum(
        "mprq,rmx->qpx",
        lax.all_gather(moved, "lon", axis=3, tiled=True),
        table,
        preferred_element_type=jnp.float32,
    ).astype(jnp.bfloat16)
    margin = REACH + 1
    tall = padded_2(grid, (("lat", 1),), margin, False)
    padded = padded_2(tall, (("lon", 2),), margin, True)
    frac_row = dep_frac[0]
    frac_col = dep_frac[1]
    col_weights = [shift_weight(dep_dlon, frac_col, shift) for shift in range(-REACH, REACH + 2)]
    total = jnp.zeros((level_fields, row_count, sector_width), jnp.float32)
    for row_shift in range(-REACH, REACH + 2):
        band = padded[:, margin + row_shift : margin + row_shift + row_count, :]
        along = jnp.zeros((level_fields, row_count, sector_width), jnp.float32)
        for place, col_shift in enumerate(range(-REACH, REACH + 2)):
            window = band[:, :, margin + col_shift : margin + col_shift + sector_width].astype(
                jnp.float32
            )
            along = along + col_weights[place][None] * window
        total = total + shift_weight(dep_drow, frac_row, row_shift)[None] * along
    return (grid, total.astype(jnp.bfloat16))


def solution(mesh):
    in_specs = (
        P(("lat", "lon"), None, None, None),
        P(("lat", "lon"), None, None),
        P(),
        P("lat", "lon"),
        P("lat", "lon"),
        P(None, "lat", "lon"),
    )
    out_specs = (P(None, "lat", "lon"), P(None, "lat", "lon"))
    return jax.shard_map(
        per_device, mesh=mesh, in_specs=in_specs, out_specs=out_specs, check_vma=False
    )
```

profile of v0, /device:TPU:5, one launch (start us, length us, event | category | flops | bytes accessed | tf_op | source)
XLA Modules:
  0.0 315.4 jit_solution(18104308854111554694)
XLA Ops:
  7.2 0.0 all-gather.2.cloned.1.call-start
  7.2 0.8 dynamic_slice.3
  8.0 0.1 iota_compare_fusion
  8.1 7.0 %broadcast_select_fusion = bf16[40,2,64,1280]{3,2,1,0:T(8,128)(2,1)S(1)} fusion(bf16[40,2,64,1280]{3,2,1,0:T(8,128)(2,1)} %param.6, pred[40,1280]{1,0:T(8,128)(4,1)S(1)} %iota_compare_fusion), kind=kLoop, calls=%fused_computation | loop fusion | flops 6553600 | bytes 26265600 | tf_op jit(solution)/shard_map/jit(_where)/select_n | solution.py:56
  15.1 19.7 %convert_bitcast_fusion = bf16[40,8,4,16,2,16]{3,5,1,2,4,0:T(8,128)(2,1)} fusion(bf16[40,2,4,16,1280,1]{4,3,5,2,1,0:T(8,128)(2,1)S(1)} %bitcast.93, bf16[40,8,16,1280,1,1]{3,2,1,5,4,0:T(8,128)(2,1)} %bitcast.97), kind=kOutput, calls=%fused_computation.1 | convolution fusion | flops 1678376960 | bytes 27525120 | tf_op jit(solution)/shard_map/mrbqn,mapn->mabprq/dot_general | solution.py:59
  34.9 17.7 %copy.20 = bf16[40,8,4,16,2,16]{0,5,4,3,2,1:T(8,128)(2,1)} copy(bf16[40,8,4,16,2,16]{3,5,1,2,4,0:T(8,128)(2,1)} %convert_bitcast_fusion) | data formatting | bytes 2621440 | tf_op jit(solution)/shard_map/convert_element_type | solution.py:61
  52.6 8.1 %reshape.245 = bf16[8,2,40960]{2,1,0:T(2,128)(2,1)S(1)} reshape(bf16[8,4,16,2,16,40]{5,4,3,2,1,0:T(8,128)(2,1)} %bitcast.92) | data formatting | bytes 2621440
  60.7 20.0 %all_to_all.33 = bf16[8,2,40960]{2,1,0:T(2,128)(2,1)S(1)} all-to-all(bf16[8,2,40960]{2,1,0:T(2,128)(2,1)S(1)} %reshape.245), channel_id=1, replica_groups=mesh['lat'=8,'lon'=4] {'lat'}, dimensions={0} | all-to-all | bytes 2621440 | tf_op jit(solution)/shard_map/all_to_all | solution.py:63
  80.7 7.2 %reshape.246 = bf16[8,4,16,2,16,40]{5,4,3,2,1,0:T(8,128)(2,1)} reshape(bf16[8,2,40960]{2,1,0:T(2,128)(2,1)S(1)} %all_to_all.33) | data formatting | bytes 2621440
  87.9 3.0 bitcast_bitcast_fusion
  90.9 6.8 %copy.21 = bf16[8,40,1,4,16,2,16]{1,0,6,5,4,3,2:T(8,128)(2,1)} copy(bf16[8,40,1,4,16,2,16]{1,6,5,4,3,0,2:T(8,128)(2,1)S(1)} %bitcast_bitcast_fusion) | data formatting | bytes 2621440 | tf_op jit(solution)/shard_map/all_to_all | solution.py:63
  97.7 5.5 %all_to_all.27 = bf16[320,1,4,16,2,16]{0,5,4,3,2,1:T(8,128)(2,1)S(1)} reshape(bf16[8,40,1,4,16,2,16]{1,0,6,5,4,3,2:T(8,128)(2,1)} %copy.21) | data formatting | bytes 2621440 | tf_op jit(solution)/shard_map/all_to_all | solution.py:63
  103.2 0.0 copy-start.3
  103.2 40.5 %all_to_all.34 = bf16[320,1,4,16,2,16]{0,5,4,3,1,2:T(8,128)(2,1)S(1)} all-to-all(bf16[320,1,4,16,2,16]{0,5,4,3,1,2:T(8,128)(2,1)S(1)} %bitcast.95), channel_id=1, replica_groups=mesh['lat'=8,'lon'=4] {'lon'}, dimensions={2} | all-to-all | bytes 2621440 | tf_op jit(solution)/shard_map/all_to_all | solution.py:62
  143.8 1.2 copy.23
  145.0 2.1 reshape.240
  147.0 0.0 all-gather.2.cloned.1.call-update
  147.1 0.0 copy-done.3
  147.1 0.1 reshape.236
  147.2 0.1 reshape.237
  147.3 29.5 %multiply_convert_fusion.1 = (bf16[1,1280,1280]{2,1,0:T(8,128)(2,1)S(1)}, bf16[1,1280,1280]{2,1,0:T(8,128)(2,1)}) fusion(s32[1280]{0:T(1024)S(1)} %iota_add_fusion, s32[1280]{0:T(1024)S(1)} %reshape.237, f32[1280]{0:T(1024)S(1)} %get-tuple-element.30, f32[1280]{0:T(1024)S(1)} %get-tuple-element.31), kind=kLoop, calls=%fused_computation.10 | loop fusion | flops 21299200 | bytes 6574080 | tf_op jit(solution)/shard_map/convert
  176.8 68.7 %all-gather.2.cloned.1.call-done = bf16[1280,16,2,64]{0,3,2,1:T(8,128)(2,1)} async-done(((bf16[1280,16,2,16]{0,3,2,1:T(8,128)(2,1)}), bf16[1280,16,2,64]{0,3,2,1:T(8,128)(2,1)}) %all-gather.2.cloned.1.call-update) | async-done | bytes 5242896 | tf_op jit(solution)/shard_map/all_gather | solution.py:76
  245.6 9.9 %fusion.8 = bf16[64,16,1280]{2,0,1:T(8,128)(2,1)S(1)} fusion(bf16[1280,16,2,64]{0,3,2,1:T(8,128)(2,1)} %all-gather.2.cloned.1.call-done, bf16[1,1280,1280]{2,1,0:T(8,128)(2,1)} %get-tuple-element.29, bf16[1,1280,1280]{2,1,0:T(8,128)(2,1)S(1)} %get-tuple-element.28), kind=kOutput, calls=%fused_computation.19 | convolution fusion | flops 6725304320 | bytes 14417920 | tf_op jit(solution)/shard_map/mprq,rmx->qpx/dot_general | solution.py:74
  255.5 0.0 copy-start
  255.5 0.0 copy-start.1
  255.5 0.0 copy-start.2
  255.6 3.6 %collective-permute-start = (bf16[64,2,1280]{2,0,1:T(8,128)(2,1)S(1)}, bf16[64,2,1280]{2,0,1:T(8,128)(2,1)S(1)}, u32[]{:S(2)}, u32[]{:S(2)}) collective-permute-start(bf16[64,2,1280]{2,0,1:T(8,128)(2,1)S(1)} %get-tuple-element.14), channel_id=1, source_target_pairs={{0,4},{4,8},{8,12},{12,16},{16,20},{20,24},{24,28},{1,5},{5,9},{9,... | collective-permute-start | bytes 983048 | tf_op jit(solution)/shard_map/ppermute | solution.py:18
  259.2 1.9 collective-permute-start.1
  261.1 2.1 collective-permute-done
  263.2 4.4 %collective-permute-done.1 = bf16[64,2,1280]{2,0,1:T(8,128)(2,1)S(1)} collective-permute-done((bf16[64,2,1280]{2,0,1:T(8,128)(2,1)S(1)}, bf16[64,2,1280]{2,0,1:T(8,128)(2,1)S(1)}, u32[]{:S(2)}, u32[]{:S(2)}) %collective-permute-start.1) | collective-permute-done | bytes 327712 | tf_op jit(solution)/shard_map/ppermute | solution.py:20
  267.6 0.2 pad_maximum_fusion.5
  267.8 0.1 collective-permute-start.2
  267.8 3.3 %collective-permute-start.3 = (bf16[64,20,2]{2,0,1:T(8,128)(2,1)S(1)}, bf16[64,20,2]{2,0,1:T(8,128)(2,1)S(1)}, u32[]{:S(2)}, u32[]{:S(2)}) collective-permute-start(bf16[64,20,2]{2,0,1:T(8,128)(2,1)S(1)} %get-tuple-element.13), channel_id=1, source_target_pairs={{1,0},{2,1},{3,2},{0,3},{5,4},{6,5},{7,6},{4,7},{9,8},{10,9},{11,1... | collective-permute-start | bytes 15368 | tf_op jit(solution)/shard_map/ppermute | solution.py:20
  271.1 0.0 copy-done
  271.1 0.0 copy-done.1
  271.1 0.0 copy-done.2
  271.1 0.1 fusion.14
  271.2 2.9 copy.24
  274.1 5.1 %collective-permute-done.2 = bf16[64,20,2]{2,0,1:T(8,128)(2,1)S(1)} collective-permute-done((bf16[64,20,2]{2,0,1:T(8,128)(2,1)S(1)}, bf16[64,20,2]{2,0,1:T(8,128)(2,1)S(1)}, u32[]{:S(2)}, u32[]{:S(2)}) %collective-permute-start.2) | collective-permute-done | bytes 5152 | tf_op jit(solution)/shard_map/ppermute | solution.py:18
  279.3 5.5 %collective-permute-done.3 = bf16[64,20,2]{2,0,1:T(8,128)(2,1)S(1)} collective-permute-done((bf16[64,20,2]{2,0,1:T(8,128)(2,1)S(1)}, bf16[64,20,2]{2,0,1:T(8,128)(2,1)S(1)}, u32[]{:S(2)}, u32[]{:S(2)}) %collective-permute-start.3) | collective-permute-done | bytes 5152 | tf_op jit(solution)/shard_map/ppermute | solution.py:20
  284.8 2.7 maximum_maximum_fusion
  287.5 18.1 %add_convert_fusion = bf16[64,16,1280]{2,0,1:T(8,128)(2,1)S(1)} fusion(bf16[64,16,1280]{2,0,1:T(8,128)(2,1)S(1)} %fusion.8, bf16[64,2,1280]{2,0,1:T(8,128)(2,1)S(1)} %collective-permute-done.1, bf16[64,20,1282]{2,0,1:T(8,128)(2,1)S(1)} %get-tuple-element.11, bf16[64,20,1282]{2,0,1:T(8,128)(2,1)S(1)} %get-tuple-element.10, ...), kind=kLoop, calls=%fused_computation.16 | loop fusion | flops 72089600 | bytes 38010880 | tf_op jit(solution)/shard_map/convert_element_type | solution.py:96
  305.6 2.9 copy.25
  (4 shorter events, 0.1 us)
Async XLA Ops:
  7.2 238.4 %all-gather.2.cloned.1.call-start = ((), (), s32[]{:S(2)}) async-start(), calls=%async_computation.2 | async-start | bytes 6553600 | tf_op jit(solution)/shard_map/all_gather | solution.py:76
  103.2 43.8 %copy-start.3 = (s32[1280]{0:T(1024)S(1)}, s32[1280]{0:T(1024)}, u32[]{:S(2)}) copy-start(s32[1280]{0:T(1024)} %param.8) | copy-start | bytes 15364
  255.5 15.6 %copy-start = (f32[2,16,1280]{2,1,0:T(8,128)S(1)}, f32[2,16,1280]{2,1,0:T(8,128)}, u32[]{:S(2)}) copy-start(f32[2,16,1280]{2,1,0:T(8,128)} %param.11) | copy-start | bytes 491524
  255.5 15.6 %copy-start.1 = (s32[16,1280]{1,0:T(8,128)S(1)}, s32[16,1280]{1,0:T(8,128)}, u32[]{:S(2)}) copy-start(s32[16,1280]{1,0:T(8,128)} %param.9) | copy-start | bytes 245764
  255.5 15.6 %copy-start.2 = (s32[16,1280]{1,0:T(8,128)S(1)}, s32[16,1280]{1,0:T(8,128)}, u32[]{:S(2)}) copy-start(s32[16,1280]{1,0:T(8,128)} %param.10) | copy-start | bytes 245764
  255.6 7.6 %collective-permute-start = (bf16[64,2,1280]{2,0,1:T(8,128)(2,1)S(1)}, bf16[64,2,1280]{2,0,1:T(8,128)(2,1)S(1)}, u32[]{:S(2)}, u32[]{:S(2)}) collective-permute-start(bf16[64,2,1280]{2,0,1:T(8,128)(2,1)S(1)} %get-tuple-element.14), channel_id=1, source_target_pairs={{0,4},{4,8},{8,12},{12,16},{16,20},{20,24},{24,28},{1,5},{5,9},{9,... | collective-permute-start | bytes 983048 | tf_op jit(solution)/shard_map/ppermute | solution.py:18
  259.2 8.4 %collective-permute-start.1 = (bf16[64,2,1280]{2,0,1:T(8,128)(2,1)S(1)}, bf16[64,2,1280]{2,0,1:T(8,128)(2,1)S(1)}, u32[]{:S(2)}, u32[]{:S(2)}) collective-permute-start(bf16[64,2,1280]{2,0,1:T(8,128)(2,1)S(1)} %get-tuple-element.15), channel_id=1, source_target_pairs={{4,0},{8,4},{12,8},{16,12},{20,16},{24,20},{28,24},{5,1},{9,5},{13... | collective-permute-start | bytes 983048 | tf_op jit(solution)/shard_map/ppermute | solution.py:20
  267.8 11.5 %collective-permute-start.2 = (bf16[64,20,2]{2,0,1:T(8,128)(2,1)S(1)}, bf16[64,20,2]{2,0,1:T(8,128)(2,1)S(1)}, u32[]{:S(2)}, u32[]{:S(2)}) collective-permute-start(bf16[64,20,2]{2,0,1:T(8,128)(2,1)S(1)} %get-tuple-element.12), channel_id=1, source_target_pairs={{0,1},{1,2},{2,3},{3,0},{4,5},{5,6},{6,7},{7,4},{8,9},{9,10},{10,1... | collective-permute-start | bytes 15368 | tf_op jit(solution)/shard_map/ppermute | solution.py:18
  267.8 16.9 %collective-permute-start.3 = (bf16[64,20,2]{2,0,1:T(8,128)(2,1)S(1)}, bf16[64,20,2]{2,0,1:T(8,128)(2,1)S(1)}, u32[]{:S(2)}, u32[]{:S(2)}) collective-permute-start(bf16[64,20,2]{2,0,1:T(8,128)(2,1)S(1)} %get-tuple-element.13), channel_id=1, source_target_pairs={{1,0},{2,1},{3,2},{0,3},{5,4},{6,5},{7,6},{4,7},{9,8},{10,9},{11,1... | collective-permute-start | bytes 15368 | tf_op jit(solution)/shard_map/ppermute | solution.py:20
Sparse Core Ops, SparseCore 0:
  147.2 98.3 all-gather.1
where the time goes:
time: 316 us; the launch traced here: 315 us
  waiting for transfers between devices  85.9 us (27%)
  blocking collectives  60.6 us (19%)
  local copies, waits for them, and re-layouts  58.5 us (19%)
  other arithmetic  57.8 us (18%)
  matrix products  29.6 us (9%)
  between operations  14.2 us (4%)
  starting transfers between devices  8.87 us (3%)
    all_gather x1, waiting for transfers between devices, per_device(): lax.all_gather(moved, 'lon', axis=3, tiled=True)  68.7 us
    all_to_all x1, blocking collectives, per_device(): lax.all_to_all(lax.all_to_all(fourier, 'lat', split_axis=1, concat_axis=0...  40.5 us
    another operation x1, other arithmetic  29.5 us
    unnamed x12, local copies, waits for them, and re-layouts  21.2 us
    all_to_all x1, blocking collectives, per_device(): lax.all_to_all(fourier, 'lat', split_axis=1, concat_axis=0, tiled=True)  20 us
    dot_general x1, matrix products, per_device(): jnp.einsum('mrbqn,mapn->mabprq', kept, matrices, preferred_element_type=j...  19.7 us
    convert_element_type x1, other arithmetic, per_device(): return (grid, total.astype(jnp.bfloat16))  18.1 us
    convert_element_type x1, local copies, waits for them, and re-layouts, per_device(): fourier = jnp.einsum('mrbqn,mapn->mabprq', kept, matrices, preferred_elem...  17.7 us
  transfers between devices with their start and end apart: 5, of which 5 were waited for; matrix products, arithmetic and copies ran while one was open for 10% of the time, Pallas kernels for 0%

commit v1 on v0

--- a/solution.py
+++ b/solution.py
@@ -5,6 +5,25 @@
 from jax.sharding import PartitionSpec as P
 
 REACH = 1
+
+
+def joined_along(blocks, dim):
+    shape = list(blocks.shape[1:])
+    shape[dim] *= blocks.shape[0]
+    return jnp.moveaxis(blocks, 0, dim).reshape(shape)
+
+
+def on_each_block(array, axis, dim, work, out_dim):
+    length, index, rows = (lax.axis_size(axis), lax.axis_index(axis), array.shape[dim])
+    right = [(i, (i + 1) % length) for i in range(length)]
+    blocks = []
+    held = array
+    for step in range(length):
+        coming = held if step == length - 1 else lax.ppermute(held, axis, right)
+        blocks.append(work(held, (index - step) % length * rows))
+        held = coming
+    blocks = jnp.stack(blocks)[(index - jnp.arange(length)) % length]
+    return joined_along(blocks, out_dim)
 
 
 def padded_2(cells, sides, width, closed):
@@ -71,11 +90,14 @@
     )
     moved = moved.reshape(all_waves, row_count, 2, quarter)
     table = wave_table(wave_order, lax.axis_index("lon") * sector_width, sector_width, cycle_size)
-    grid = jnp.einsum(
-        "mprq,rmx->qpx",
-        lax.all_gather(moved, "lon", axis=3, tiled=True),
-        table,
-        preferred_element_type=jnp.float32,
+    grid = on_each_block(
+        moved,
+        "lon",
+        3,
+        lambda own_block, start: jnp.einsum(
+            "mprq,rmx->qpx", own_block, table, preferred_element_type=jnp.float32
+        ),
+        0,
     ).astype(jnp.bfloat16)
     margin = REACH + 1
     tall = padded_2(grid, (("lat", 1),), margin, False)

time: 316 us -> 306 us (0.968)
  blocking collectives: 60.6 us -> 0 us
  waiting for transfers between devices: 85.9 us -> 123 us
  starting transfers between devices: 8.87 us -> 22.9 us
  between operations: 14.2 us -> 0.86 us
  other arithmetic: 57.8 us -> 67.3 us
    ppermute x0 -> x3, waiting for transfers between devices: none -> 79.2 us  [on_each_block(): coming = held if step == length - 1 else lax.ppermute(held, axis, right)]
    all_gather x1 -> x0, waiting for transfers between devices: 68.7 us -> none  [per_device(): lax.all_gather(moved, 'lon', axis=3, tiled=True)]
    all_to_all x2 -> x0, blocking collectives: 60.6 us -> none  [the longest x1 40.5 us: per_device(): lax.all_to_all(lax.all_to_all(fourier, 'lat', split_axis=1, concat_axis=0...]
    all_to_all x0 -> x2, waiting for transfers between devices: none -> 21 us  [the longest x1 14.3 us: per_device(): lax.all_to_all(fourier, 'lat', split_axis=1, concat_axis=0, tiled=True)]
    all_to_all x0 -> x2, starting transfers between devices: none -> 9.12 us  [the longest x1 4.58 us: per_device(): lax.all_to_all(fourier, 'lat', split_axis=1, concat_axis=0, tiled=True)]
    ppermute x2, waiting for transfers between devices: 7.2 us -> 12.4 us  [padded_2(): lax.ppermute(tail, axis, [(i, (i + 1) % count) for i in range(ends)])]
    unnamed x12 -> x16, local copies, waits for them, and re-layouts: 21.2 us -> 16.2 us
    ppermute x2, starting transfers between devices: 3.66 us -> 8.32 us  [padded_2(): lax.ppermute(tail, axis, [(i, (i + 1) % count) for i in range(ends)])]
  transfers between devices with their start and end apart: 5 -> 9, of which waited for: 5 -> 9; matrix products, arithmetic and copies ran while one was open for 10% -> 13% of each run, Pallas kernels for 0% -> 0%
where the time goes in v1:
time: 306 us; the launch traced here: 305 us
  waiting for transfers between devices  123 us (40%)
  other arithmetic  67.3 us (22%)
  local copies, waits for them, and re-layouts  58.6 us (19%)
  matrix products  32 us (10%)
  starting transfers between devices  22.9 us (7%)
    ppermute x3, waiting for transfers between devices, on_each_block(): coming = held if step == length - 1 else lax.ppermute(held, axis, right)  79.2 us
    another operation x1, other arithmetic  29.7 us
    convert_element_type x1, other arithmetic, per_device(): return (grid, total.astype(jnp.bfloat16))  22.5 us
    dot_general x1, matrix products, per_device(): jnp.einsum('mrbqn,mapn->mabprq', kept, matrices, preferred_element_type=j...  19.7 us
    convert_element_type x1, local copies, waits for them, and re-layouts, per_device(): fourier = jnp.einsum('mrbqn,mapn->mabprq', kept, matrices, preferred_elem...  17.7 us
    unnamed x16, local copies, waits for them, and re-layouts  16.2 us
    all_to_all x3, local copies, waits for them, and re-layouts, per_device(): lax.all_to_all(fourier, 'lat', split_axis=1, concat_axis=0, tiled=True)  16.1 us
    all_to_all x1, waiting for transfers between devices, per_device(): lax.all_to_all(fourier, 'lat', split_axis=1, concat_axis=0, tiled=True)  14.3 us
  transfers between devices with their start and end apart: 9, of which 9 were waited for; matrix products, arithmetic and copies ran while one was open for 13% of the time, Pallas kernels for 0%

profile of v1, /device:TPU:5, one launch (start us, length us, event | category | flops | bytes accessed | tf_op | source)
XLA Modules:
  0.0 304.8 jit_solution(1666190829812416695)
XLA Ops:
  0.6 0.8 dynamic_slice.3
  1.4 0.1 iota_compare_fusion
  1.5 7.0 %broadcast_select_fusion = bf16[40,2,64,1280]{3,2,1,0:T(8,128)(2,1)S(1)} fusion(bf16[40,2,64,1280]{3,2,1,0:T(8,128)(2,1)} %param.6, pred[40,1280]{1,0:T(8,128)(4,1)S(1)} %iota_compare_fusion), kind=kLoop, calls=%fused_computation.1 | loop fusion | flops 6553600 | bytes 26265600 | tf_op jit(solution)/shard_map/jit(_where)/select_n | solution.py:75
  8.5 19.7 %convert_bitcast_fusion = bf16[40,8,4,16,2,16]{3,5,1,2,4,0:T(8,128)(2,1)} fusion(bf16[40,2,4,16,1280,1]{4,3,5,2,1,0:T(8,128)(2,1)S(1)} %bitcast.127, bf16[40,8,16,1280,1,1]{3,2,1,5,4,0:T(8,128)(2,1)} %bitcast.130), kind=kOutput, calls=%fused_computation.2 | convolution fusion | flops 1678376960 | bytes 27525120 | tf_op jit(solution)/shard_map/mrbqn,mapn->mabprq/dot_general | solution.py:78
  28.3 17.7 %copy.16 = bf16[40,8,4,16,2,16]{0,5,4,3,2,1:T(8,128)(2,1)} copy(bf16[40,8,4,16,2,16]{3,5,1,2,4,0:T(8,128)(2,1)} %convert_bitcast_fusion) | data formatting | bytes 2621440 | tf_op jit(solution)/shard_map/convert_element_type | solution.py:80
  45.9 0.0 copy-start.6
  45.9 9.0 %reshape.307 = bf16[8,2,40960]{2,1,0:T(2,128)(2,1)} reshape(bf16[8,4,16,2,16,40]{5,4,3,2,1,0:T(8,128)(2,1)} %bitcast.126) | data formatting | bytes 2621440
  54.9 4.6 %all-to-all-start = ((bf16[8,2,40960]{2,1,0:T(2,128)(2,1)}), bf16[8,2,40960]{2,1,0:T(2,128)(2,1)S(1)}, u32[]{:S(2)}, u32[]{:S(2)}) async-start(bf16[8,2,40960]{2,1,0:T(2,128)(2,1)} %reshape.307), calls=%async_computation | async-start | bytes 2621440 | tf_op jit(solution)/shard_map/all_to_all | solution.py:82
  59.5 0.0 copy-done.6
  59.5 0.1 reshape.287
  59.6 0.1 reshape.288
  59.7 14.3 %all-to-all-done = bf16[8,2,40960]{2,1,0:T(2,128)(2,1)S(1)} async-done(((bf16[8,2,40960]{2,1,0:T(2,128)(2,1)}), bf16[8,2,40960]{2,1,0:T(2,128)(2,1)S(1)}, u32[]{:S(2)}, u32[]{:S(2)}) %all-to-all-start) | async-done | bytes 1310752 | tf_op jit(solution)/shard_map/all_to_all | solution.py:82
  74.0 7.1 %reshape.308 = bf16[8,4,16,2,16,40]{5,4,3,2,1,0:T(8,128)(2,1)} reshape(bf16[8,2,40960]{2,1,0:T(2,128)(2,1)S(1)} %all-to-all-done) | data formatting | bytes 2621440
  81.1 3.0 bitcast_bitcast_fusion
  84.1 6.8 %copy.17 = bf16[8,40,1,4,16,2,16]{1,0,6,5,4,3,2:T(8,128)(2,1)} copy(bf16[8,40,1,4,16,2,16]{1,6,5,4,3,0,2:T(8,128)(2,1)S(1)} %bitcast_bitcast_fusion) | data formatting | bytes 2621440 | tf_op jit(solution)/shard_map/all_to_all | solution.py:82
  90.9 6.4 %all_to_all.27 = bf16[320,1,4,16,2,16]{0,5,4,3,2,1:T(8,128)(2,1)} reshape(bf16[8,40,1,4,16,2,16]{1,0,6,5,4,3,2:T(8,128)(2,1)} %copy.17) | data formatting | bytes 2621440 | tf_op jit(solution)/shard_map/all_to_all | solution.py:82
  97.2 4.5 %all-to-all-start.1 = ((bf16[320,1,4,16,2,16]{0,5,4,3,1,2:T(8,128)(2,1)}), bf16[320,1,4,16,2,16]{0,5,4,3,1,2:T(8,128)(2,1)S(1)}, u32[]{:S(2)}, u32[]{:S(2)}) async-start(bf16[320,1,4,16,2,16]{0,5,4,3,1,2:T(8,128)(2,1)} %bitcast.9), calls=%async_computation.1 | async-start | bytes 3145728 | tf_op jit(solution)/shard_map/all_to_all | solution.py:81
  101.8 29.7 %multiply_convert_fusion.1 = (bf16[1,1280,1280]{2,1,0:T(8,128)(2,1)}, bf16[1,1280,1280]{2,1,0:T(8,128)(2,1)}) fusion(s32[1280]{0:T(1024)S(1)} %iota_add_fusion, s32[1280]{0:T(1024)S(1)} %reshape.288, f32[1280]{0:T(1024)S(1)} %get-tuple-element.22, f32[1280]{0:T(1024)S(1)} %get-tuple-element.23), kind=kLoop, calls=%fused_computation.8 | loop fusion | flops 21299200 | bytes 6574080 | tf_op jit(solution)/shard_map/convert
  131.5 6.8 %all-to-all-done.1 = bf16[320,1,4,16,2,16]{0,5,4,3,1,2:T(8,128)(2,1)S(1)} async-done(((bf16[320,1,4,16,2,16]{0,5,4,3,1,2:T(8,128)(2,1)}), bf16[320,1,4,16,2,16]{0,5,4,3,1,2:T(8,128)(2,1)S(1)}, u32[]{:S(2)}, u32[]{:S(2)}) %all-to-all-start.1) | async-done | bytes 1310752 | tf_op jit(solution)/shard_map/all_to_all | solution.py:81
  138.2 1.2 copy.19
  139.5 1.2 reshape.291
  140.7 0.3 collective-permute-start
  141.0 0.0 copy-start.1
  141.0 0.0 copy-start.2
  141.0 4.9 %convolution_bitcast_fusion.3 = bf16[1,16,16,1280]{3,1,2,0:T(8,128)(2,1)S(1)} fusion(bf16[1280,16,2,16]{0,3,2,1:T(8,128)(2,1)S(1)} %reshape.291, bf16[1,1280,1280]{2,1,0:T(8,128)(2,1)} %get-tuple-element.21, bf16[1,1280,1280]{2,1,0:T(8,128)(2,1)} %get-tuple-element.20), kind=kOutput, calls=%fused_computation.22 | convolution fusion | flops 1690828800 | bytes 8519680 | tf_op jit(solution)/shard_map/mprq,rmx->qpx/dot_general | solution.py:97
  146.0 25.6 %collective-permute-done = bf16[1280,16,2,16]{0,3,2,1:T(8,128)(2,1)S(1)} collective-permute-done((bf16[1280,16,2,16]{0,3,2,1:T(8,128)(2,1)S(1)}, bf16[1280,16,2,16]{0,3,2,1:T(8,128)(2,1)S(1)}, u32[]{:S(2)}, u32[]{:S(2)}) %collective-permute-start) | collective-permute-done | bytes 1310752 | tf_op jit(solution)/shard_map/ppermute | solution.py:22
  171.6 0.0 collective-permute-start.1
  171.6 0.0 copy-done.1
  171.6 0.0 copy-done.2
  171.6 2.5 convolution_bitcast_fusion.2
  174.1 27.2 %collective-permute-done.1 = bf16[1280,16,2,16]{0,3,2,1:T(8,128)(2,1)S(1)} collective-permute-done((bf16[1280,16,2,16]{0,3,2,1:T(8,128)(2,1)S(1)}, bf16[1280,16,2,16]{0,3,2,1:T(8,128)(2,1)S(1)}, u32[]{:S(2)}, u32[]{:S(2)}) %collective-permute-start.1) | collective-permute-done | bytes 1310752 | tf_op jit(solution)/shard_map/ppermute | solution.py:22
  201.3 0.0 collective-permute-start.2
  201.3 2.4 convolution_bitcast_fusion.1
  203.7 26.3 %collective-permute-done.2 = bf16[1280,16,2,16]{0,3,2,1:T(8,128)(2,1)S(1)} collective-permute-done((bf16[1280,16,2,16]{0,3,2,1:T(8,128)(2,1)S(1)}, bf16[1280,16,2,16]{0,3,2,1:T(8,128)(2,1)S(1)}, u32[]{:S(2)}, u32[]{:S(2)}) %collective-permute-start.2) | collective-permute-done | bytes 1310752 | tf_op jit(solution)/shard_map/ppermute | solution.py:22
  230.0 2.4 convolution_bitcast_fusion
  232.5 0.3 pad_maximum_fusion
  232.8 2.2 gather_fusion
  235.0 0.0 copy-start.3
  235.0 0.0 copy-start.4
  235.0 0.0 copy-start.5
  235.1 2.6 copy.20
  237.6 0.0 copy-start
  237.7 0.5 fusion.17
  238.2 8.3 %collective-permute-start.3 = (bf16[64,2,1280]{2,1,0:T(2,128)(2,1)S(1)}, bf16[64,2,1280]{2,1,0:T(2,128)(2,1)S(1)}, u32[]{:S(2)}, u32[]{:S(2)}) collective-permute-start(bf16[64,2,1280]{2,1,0:T(2,128)(2,1)S(1)} %get-tuple-element.6), channel_id=1, source_target_pairs={{0,4},{4,8},{8,12},{12,16},{16,20},{20,24},{24,28},{1,5},{5,9},{9,... | collective-permute-start | bytes 983048 | tf_op jit(solution)/shard_map/ppermute | solution.py:37
  246.4 1.9 collective-permute-start.4
  248.4 2.9 collective-permute-done.3
  251.3 3.6 %collective-permute-done.4 = bf16[64,2,1280]{2,1,0:T(2,128)(2,1)S(1)} collective-permute-done((bf16[64,2,1280]{2,1,0:T(2,128)(2,1)S(1)}, bf16[64,2,1280]{2,1,0:T(2,128)(2,1)S(1)}, u32[]{:S(2)}, u32[]{:S(2)}) %collective-permute-start.4) | collective-permute-done | bytes 327712 | tf_op jit(solution)/shard_map/ppermute | solution.py:39
  254.8 0.5 pad_maximum_fusion.6
  255.3 0.1 collective-permute-start.5
  255.4 3.3 %collective-permute-start.6 = (bf16[64,20,2]{2,1,0:T(8,128)(2,1)S(1)}, bf16[64,20,2]{2,1,0:T(8,128)(2,1)S(1)}, u32[]{:S(2)}, u32[]{:S(2)}) collective-permute-start(bf16[64,20,2]{2,1,0:T(8,128)(2,1)S(1)} %get-tuple-element.5), channel_id=1, source_target_pairs={{1,0},{2,1},{3,2},{0,3},{5,4},{6,5},{7,6},{4,7},{9,8},{10,9},{11,1... | collective-permute-start | bytes 15368 | tf_op jit(solution)/shard_map/ppermute | solution.py:39
  258.7 0.0 copy-done.3
  258.7 0.0 copy-done.4
  258.7 0.0 copy-done.5
  258.7 0.1 fusion.10
  258.8 9.5 %collective-permute-done.5 = bf16[64,20,2]{2,1,0:T(8,128)(2,1)S(1)} collective-permute-done((bf16[64,20,2]{2,1,0:T(8,128)(2,1)S(1)}, bf16[64,20,2]{2,1,0:T(8,128)(2,1)S(1)}, u32[]{:S(2)}, u32[]{:S(2)}) %collective-permute-start.5) | collective-permute-done | bytes 5152 | tf_op jit(solution)/shard_map/ppermute | solution.py:37
  268.3 6.9 %collective-permute-done.6 = bf16[64,20,2]{2,1,0:T(8,128)(2,1)S(1)} collective-permute-done((bf16[64,20,2]{2,1,0:T(8,128)(2,1)S(1)}, bf16[64,20,2]{2,1,0:T(8,128)(2,1)S(1)}, u32[]{:S(2)}, u32[]{:S(2)}) %collective-permute-start.6) | collective-permute-done | bytes 5152 | tf_op jit(solution)/shard_map/ppermute | solution.py:39
  275.2 7.0 %maximum_maximum_fusion = (bf16[64,20,1282]{2,1,0:T(8,128)(2,1)S(1)}, bf16[64,20,1282]{2,1,0:T(8,128)(2,1)S(1)}) fusion(bf16[64,2,1280]{2,1,0:T(2,128)(2,1)S(1)} %collective-permute-done.4, bf16[64,16,1280]{2,1,0:T(8,128)(2,1)S(1)} %bitcast.123, bf16[64,2,1280]{2,1,0:T(2,128)(2,1)S(1)} %collective-permute-done.3, ...), kind=kLoop, calls=%fused_computation.15 | loop fusion | flops 26255360 | bytes 9850880 | tf_op jit(solution)/shard_map/concatenate | solution.py:35
  282.3 0.0 copy-done
  282.3 22.5 %add_convert_fusion = bf16[64,16,1280]{2,1,0:T(8,128)(2,1)} fusion(bf16[64,16,1280]{2,1,0:T(8,128)(2,1)S(1)} %bitcast.124, bf16[64,2,1280]{2,1,0:T(2,128)(2,1)S(1)} %collective-permute-done.4, bf16[64,20,1282]{2,1,0:T(8,128)(2,1)S(1)} %get-tuple-element.3, bf16[64,20,1282]{2,1,0:T(8,128)(2,1)S(1)} %get-tuple-element.2, ...), kind=kLoop, calls=%fused_computation.14 | loop fusion | flops 79953920 | bytes 38010880 | tf_op jit(solution)/shard_map/convert_element_type | solution.py:118
  (5 shorter events, 0.0 us)
Async XLA Ops:
  45.9 13.6 %copy-start.6 = (s32[1280]{0:T(1024)S(1)}, s32[1280]{0:T(1024)}, u32[]{:S(2)}) copy-start(s32[1280]{0:T(1024)} %param.8) | copy-start | bytes 15364
  54.9 19.1 %all-to-all-start = ((bf16[8,2,40960]{2,1,0:T(2,128)(2,1)}), bf16[8,2,40960]{2,1,0:T(2,128)(2,1)S(1)}, u32[]{:S(2)}, u32[]{:S(2)}) async-start(bf16[8,2,40960]{2,1,0:T(2,128)(2,1)} %reshape.307), calls=%async_computation | async-start | bytes 2621440 | tf_op jit(solution)/shard_map/all_to_all | solution.py:82
  97.2 41.0 %all-to-all-start.1 = ((bf16[320,1,4,16,2,16]{0,5,4,3,1,2:T(8,128)(2,1)}), bf16[320,1,4,16,2,16]{0,5,4,3,1,2:T(8,128)(2,1)S(1)}, u32[]{:S(2)}, u32[]{:S(2)}) async-start(bf16[320,1,4,16,2,16]{0,5,4,3,1,2:T(8,128)(2,1)} %bitcast.9), calls=%async_computation.1 | async-start | bytes 3145728 | tf_op jit(solution)/shard_map/all_to_all | solution.py:81
  140.7 30.9 %collective-permute-start = (bf16[1280,16,2,16]{0,3,2,1:T(8,128)(2,1)S(1)}, bf16[1280,16,2,16]{0,3,2,1:T(8,128)(2,1)S(1)}, u32[]{:S(2)}, u32[]{:S(2)}) collective-permute-start(bf16[1280,16,2,16]{0,3,2,1:T(8,128)(2,1)S(1)} %reshape.291), channel_id=1, source_target_pairs={{0,1},{1,2},{2,3},{3,0},{4,5},{5,6},{6,7},{7,4},{8,9},{9,10},{10,1... | collective-permute-start | bytes 3932168 | tf_op jit(solution)/shard_map/ppermute | solution.py:22
  141.0 30.6 %copy-start.1 = (bf16[1,1280,1280]{2,1,0:T(8,128)(2,1)S(1)}, bf16[1,1280,1280]{2,1,0:T(8,128)(2,1)}, u32[]{:S(2)}) copy-start(bf16[1,1280,1280]{2,1,0:T(8,128)(2,1)} %get-tuple-element.20) | copy-start | bytes 9830404
  141.0 30.6 %copy-start.2 = (bf16[1,1280,1280]{2,1,0:T(8,128)(2,1)S(1)}, bf16[1,1280,1280]{2,1,0:T(8,128)(2,1)}, u32[]{:S(2)}) copy-start(bf16[1,1280,1280]{2,1,0:T(8,128)(2,1)} %get-tuple-element.21) | copy-start | bytes 9830404
  171.6 29.7 %collective-permute-start.1 = (bf16[1280,16,2,16]{0,3,2,1:T(8,128)(2,1)S(1)}, bf16[1280,16,2,16]{0,3,2,1:T(8,128)(2,1)S(1)}, u32[]{:S(2)}, u32[]{:S(2)}) collective-permute-start(bf16[1280,16,2,16]{0,3,2,1:T(8,128)(2,1)S(1)} %collective-permute-done), channel_id=1, source_target_pairs={{0,1},{1,2},{2,3},{3,0},{4,5},{5,6},{6,7},{7,4},{8,9},{9,10},{10,1... | collective-permute-start | bytes 3932168 | tf_op jit(solution)/shard_map/ppermute | solution.py:22
  201.3 28.8 %collective-permute-start.2 = (bf16[1280,16,2,16]{0,3,2,1:T(8,128)(2,1)S(1)}, bf16[1280,16,2,16]{0,3,2,1:T(8,128)(2,1)S(1)}, u32[]{:S(2)}, u32[]{:S(2)}) collective-permute-start(bf16[1280,16,2,16]{0,3,2,1:T(8,128)(2,1)S(1)} %collective-permute-done.1), channel_id=1, source_target_pairs={{0,1},{1,2},{2,3},{3,0},{4,5},{5,6},{6,7},{7,4},{8,9},{9,10},{10,1... | collective-permute-start | bytes 3932168 | tf_op jit(solution)/shard_map/ppermute | solution.py:22
  235.0 23.6 %copy-start.3 = (f32[2,16,1280]{2,1,0:T(8,128)S(1)}, f32[2,16,1280]{2,1,0:T(8,128)}, u32[]{:S(2)}) copy-start(f32[2,16,1280]{2,1,0:T(8,128)} %param.11) | copy-start | bytes 491524
  235.0 23.6 %copy-start.4 = (s32[16,1280]{1,0:T(8,128)S(1)}, s32[16,1280]{1,0:T(8,128)}, u32[]{:S(2)}) copy-start(s32[16,1280]{1,0:T(8,128)} %param.9) | copy-start | bytes 245764
  235.0 23.6 %copy-start.5 = (s32[16,1280]{1,0:T(8,128)S(1)}, s32[16,1280]{1,0:T(8,128)}, u32[]{:S(2)}) copy-start(s32[16,1280]{1,0:T(8,128)} %param.10) | copy-start | bytes 245764
  237.6 44.6 %copy-start = (bf16[4,16,16,1280]{3,2,1,0:T(8,128)(2,1)}, bf16[4,16,16,1280]{3,2,1,0:T(8,128)(2,1)S(1)}, u32[]{:S(2)}) copy-start(bf16[4,16,16,1280]{3,2,1,0:T(8,128)(2,1)S(1)} %copy.20) | copy-start | bytes 7864324
  238.2 13.1 %collective-permute-start.3 = (bf16[64,2,1280]{2,1,0:T(2,128)(2,1)S(1)}, bf16[64,2,1280]{2,1,0:T(2,128)(2,1)S(1)}, u32[]{:S(2)}, u32[]{:S(2)}) collective-permute-start(bf16[64,2,1280]{2,1,0:T(2,128)(2,1)S(1)} %get-tuple-element.6), channel_id=1, source_target_pairs={{0,4},{4,8},{8,12},{12,16},{16,20},{20,24},{24,28},{1,5},{5,9},{9,... | collective-permute-start | bytes 983048 | tf_op jit(solution)/shard_map/ppermute | solution.py:37
  246.4 8.4 %collective-permute-start.4 = (bf16[64,2,1280]{2,1,0:T(2,128)(2,1)S(1)}, bf16[64,2,1280]{2,1,0:T(2,128)(2,1)S(1)}, u32[]{:S(2)}, u32[]{:S(2)}) collective-permute-start(bf16[64,2,1280]{2,1,0:T(2,128)(2,1)S(1)} %get-tuple-element.7), channel_id=1, source_target_pairs={{4,0},{8,4},{12,8},{16,12},{20,16},{24,20},{28,24},{5,1},{9,5},{13... | collective-permute-start | bytes 983048 | tf_op jit(solution)/shard_map/ppermute | solution.py:39
  255.3 13.0 %collective-permute-start.5 = (bf16[64,20,2]{2,1,0:T(8,128)(2,1)S(1)}, bf16[64,20,2]{2,1,0:T(8,128)(2,1)S(1)}, u32[]{:S(2)}, u32[]{:S(2)}) collective-permute-start(bf16[64,20,2]{2,1,0:T(8,128)(2,1)S(1)} %get-tuple-element.4), channel_id=1, source_target_pairs={{0,1},{1,2},{2,3},{3,0},{4,5},{5,6},{6,7},{7,4},{8,9},{9,10},{10,1... | collective-permute-start | bytes 15368 | tf_op jit(solution)/shard_map/ppermute | solution.py:37
  255.4 19.8 %collective-permute-start.6 = (bf16[64,20,2]{2,1,0:T(8,128)(2,1)S(1)}, bf16[64,20,2]{2,1,0:T(8,128)(2,1)S(1)}, u32[]{:S(2)}, u32[]{:S(2)}) collective-permute-start(bf16[64,20,2]{2,1,0:T(8,128)(2,1)S(1)} %get-tuple-element.5), channel_id=1, source_target_pairs={{1,0},{2,1},{3,2},{0,3},{5,4},{6,5},{7,6},{4,7},{9,8},{10,9},{11,1... | collective-permute-start | bytes 15368 | tf_op jit(solution)/shard_map/ppermute | solution.py:39
